TPU v7x, 256 devices: a whole 4x4x8 slice. The times are simulated.
256 devices in a mesh: dp: 16 (over y_hi, z), seq: 16 (over x, y_lo, core).
Axes of the slice: x: 4, y: 4 (y_hi: 2, y_lo: 2; y = y_hi * 2 + y_lo), z: 8, core: 2. Of those that a mesh axis runs over, the one named last changes fastest.
Arguments:
- queries: bfloat16 [16, 2048, 2048], P('dp', 'seq'), may hold values from -6 to 6
- key_states: bfloat16 [16, 2048, 2048], P('dp', 'seq'), may hold values from -6 to 6
- value_states: bfloat16 [16, 2048, 2048], P('dp', 'seq'), may hold values from -6 to 6
- cotangent: bfloat16 [16, 2048, 2048], P('dp', 'seq'), may hold values from -6 to 6
- filter_taps: float32 [7, 2048], replicated, may hold values from -3 to 3
Outputs:
- conv_output: bfloat16 [16, 2048, 2048], P('dp', 'seq')
- grad_queries: bfloat16 [16, 2048, 2048], P('dp', 'seq')
- grad_keys: bfloat16 [16, 2048, 2048], P('dp', 'seq')
- grad_values: bfloat16 [16, 2048, 2048], P('dp', 'seq')
- filter_gradient: float32 [7, 2048], replicated
All inputs are finite; a program needn't handle non-finite values.
Results may differ from a plain program's by a relative error of at most 0.015.
Values may be sent and summed in bfloat16 or wider, within the bound.
No kernel may reach another device: no remote copies, remote signals or barrier semaphores. Data moves between devices by JAX's collectives and lax.ppermute only.
A program may use at most 128 MiB of HBM per device.

v0:
```python
import math
import jax
import jax.numpy as jnp
from jax import lax
from jax.sharding import PartitionSpec as P

HD = 128
TAPS = 7


def padded(value, sides, width):
    for axis, dim in sides:
        peers, length = (lax.axis_size(axis), value.shape[dim])
        up = [(i, (i + 1) % peers) for i in range(peers)]
        down = [(j, i) for i, j in up]
        last = lax.slice_in_dim(value, length - width, length, axis=dim)
        leading = lax.slice_in_dim(value, 0, width, axis=dim)
        before = lax.ppermute(last, axis, up)
        after = lax.ppermute(leading, axis, down)
        value = jnp.concatenate([before, value, after], axis=dim)
    return value


def on_device(queries, key_states, value_states, cotangent, filter_taps):
    tok_rows = queries.shape[1]
    channels = queries.shape[2]
    sequence_shards = lax.axis_size("seq")
    seq_total = tok_rows * sequence_shards
    head_count = channels // HD
    group_heads = math.gcd(head_count, 4)
    group_width = group_heads * HD
    group_count = head_count // group_heads
    score_scale = HD ** (-0.5)
    half_width = (TAPS - 1) // 2
    local_q = queries[0]
    local_k = key_states[0]
    local_v = value_states[0]
    local_g = cotangent[0]
    grad_pad = padded(local_g, (("seq", 0),), half_width)
    grad_sum = jnp.zeros((tok_rows, channels), jnp.float32)
    for tap_index in range(TAPS):
        start_row = 2 * half_width - tap_index
        grad_sum = grad_sum + filter_taps[tap_index] * grad_pad[
            start_row : start_row + tok_rows
        ].astype(jnp.float32)
    grad_attn = grad_sum.astype(jnp.bfloat16)
    key_all, value_all = (
        lax.all_gather(local_k, "seq", axis=0, tiled=True),
        lax.all_gather(local_v, "seq", axis=0, tiled=True),
    )
    device_index = lax.axis_index("seq")
    query_pos = device_index * tok_rows + jnp.arange(tok_rows, dtype=jnp.int32)
    key_pos = jnp.arange(seq_total, dtype=jnp.int32)
    visible = query_pos[:, None] >= key_pos[None, :]

    def columns(matrix, group_index, count):
        picked = lax.dynamic_slice_in_dim(matrix, group_index * group_width, group_width, 1)
        return picked.reshape(count, group_heads, HD)

    def forward_group(group_index):
        q_part = columns(local_q, group_index, tok_rows)
        k_part = columns(key_all, group_index, seq_total)
        v_part = columns(value_all, group_index, seq_total)
        delta_portion = columns(grad_attn, group_index, tok_rows)
        scores = (
            jnp.einsum("thd,uhd->htu", q_part, k_part, preferred_element_type=jnp.float32)
            * score_scale
        )
        row_top = jnp.max(jnp.where(visible, scores, -jnp.inf), -1, keepdims=True)
        raw = jnp.where(visible, jnp.exp(scores - row_top), 0.0)
        row_total = jnp.sum(raw, -1, keepdims=True)
        probs = raw / row_total
        probs_low = probs.astype(jnp.bfloat16)
        attended = jnp.einsum("htu,uhd->thd", probs_low, v_part, preferred_element_type=jnp.float32)
        attended = attended.astype(jnp.bfloat16).reshape(tok_rows, group_width)
        dprob = jnp.einsum(
            "thd,uhd->htu", delta_portion, v_part, preferred_element_type=jnp.float32
        )
        row_delta = jnp.sum(probs * dprob, -1, keepdims=True)
        dscore = (probs * (dprob - row_delta) * score_scale).astype(jnp.bfloat16)
        grad_q = jnp.einsum("htu,uhd->thd", dscore, k_part, preferred_element_type=jnp.float32)
        grad_q = grad_q.astype(jnp.bfloat16).reshape(tok_rows, group_width)
        key_term = jnp.einsum("htu,thd->uhd", dscore, q_part, preferred_element_type=jnp.float32)
        value_term = jnp.einsum(
            "htu,thd->uhd", probs_low, delta_portion, preferred_element_type=jnp.float32
        )
        return (
            attended,
            grad_q,
            key_term.reshape(seq_total, group_width),
            value_term.reshape(seq_total, group_width),
        )

    group_ids = jnp.arange(group_count, dtype=jnp.int32)
    attended, grad_q, key_term, value_term = lax.map(forward_group, group_ids)
    key_share, value_share = (
        lax.psum_scatter(
            key_term.astype(jnp.bfloat16), "seq", scatter_dimension=1, tiled=True
        ).astype(jnp.float32),
        lax.psum_scatter(
            value_term.astype(jnp.bfloat16), "seq", scatter_dimension=1, tiled=True
        ).astype(jnp.float32),
    )
    grad_keys = key_share.transpose(1, 0, 2).reshape(tok_rows, channels).astype(jnp.bfloat16)
    grad_values = value_share.transpose(1, 0, 2).reshape(tok_rows, channels).astype(jnp.bfloat16)
    attn_out = attended.transpose(1, 0, 2).reshape(tok_rows, channels)
    grad_queries = grad_q.transpose(1, 0, 2).reshape(tok_rows, channels)
    out_pad = padded(attn_out, (("seq", 0),), half_width)
    conv_sum = jnp.zeros((tok_rows, channels), jnp.float32)
    filter_rows = []
    local_gf = local_g.astype(jnp.float32)
    for tap_index in range(TAPS):
        moved = out_pad[tap_index : tap_index + tok_rows].astype(jnp.float32)
        conv_sum = conv_sum + filter_taps[tap_index] * moved
        filter_rows.append(jnp.sum(moved * local_gf, 0))
    filter_gradient = lax.psum(jnp.stack(filter_rows, 0), ("dp", "seq"))
    conv_output = conv_sum.astype(jnp.bfloat16)
    return (
        conv_output[None],
        grad_queries[None],
        grad_keys[None],
        grad_values[None],
        filter_gradient,
    )


def solution(mesh):
    in_specs = (
        P("dp", "seq", None),
        P("dp", "seq", None),
        P("dp", "seq", None),
        P("dp", "seq", None),
        P(),
    )
    out_specs = (
        P("dp", "seq", None),
        P("dp", "seq", None),
        P("dp", "seq", None),
        P("dp", "seq", None),
        P(),
    )
    return jax.shard_map(
        on_device, mesh=mesh, in_specs=in_specs, out_specs=out_specs, check_vma=False
    )
```

profile of v0, /device:TPU:1, one launch (start us, length us, event | category | flops | bytes accessed | tf_op | source)
XLA Modules:
  0.0 557.8 jit_solution(18201332075401801703)
XLA Ops:
  20.9 57.9 %all-gather.5.cloned.1.call-done = bf16[1,2048,2048]{1,2,0:T(8,128)(2,1)} async-done(((bf16[1,128,2048]{1,2,0:T(8,128)(2,1)}), bf16[1,2048,2048]{1,2,0:T(8,128)(2,1)}) %all-gather.5.cloned.1.call-update) | async-done | bytes 8388624 | tf_op jit(solution)/shard_map/all_gather | solution.py:49
  78.7 65.4 %all-gather.7.cloned.1.call-done = bf16[1,2048,2048]{1,2,0:T(8,128)(2,1)} async-done(((bf16[1,128,2048]{1,2,0:T(8,128)(2,1)}), bf16[1,2048,2048]{1,2,0:T(8,128)(2,1)}) %all-gather.7.cloned.1.call-update) | async-done | bytes 8388624 | tf_op jit(solution)/shard_map/all_gather | solution.py:48
  144.2 177.4 %while.17 = (s32[]{:T(128)}, bf16[4,128,512]{1,2,0:T(8,128)(2,1)S(1)}, bf16[4,128,512]{1,2,0:T(8,128)(2,1)}, bf16[4,2048,512]{1,2,0:T(8,128)(2,1)}, bf16[4,2048,...) while((s32[]{:T(128)}, ...), condition=%wide.region_4.5_spmd.clone, body=%wide.region_0.4_spmd.clone.sunk | while | flops 1904614400 | bytes 82324224 | solution.py:95
  145.5 3.2 constant_dynamic-slice_fusion.8
  155.4 6.5 %fusion.111 = (f32[4,128]{1,0:T(4,128)S(1)}, f32[4,128,2048]{2,1,0:T(8,128)}) fusion(pred[128,2048]{1,0:T(8,128)(4,1)S(1)} %iota_compare_fusion.2, bf16[128,4,128]{0,2,1:T(8,128)(2,1)S(1)} %bitcast.143, bf16[2048,4,128]{0,2,1:T(8,128)(2,1)} %bitcast.125), kind=kOutput, calls=%fused_computation.95.clone.1 | convolution fusion | flops 543164416 | bytes 6686720 | tf_op jit(solution)/shard_map/while/body/eval_jaxpr/sub | solution.py:70
  161.9 8.5 %fusion.112 = bf16[4,128,128]{2,1,0:T(8,128)(2,1)S(1)} fusion(bf16[2048,4,128]{0,2,1:T(8,128)(2,1)} %bitcast.126, f32[4,128,2048]{2,1,0:T(8,128)} %fusion.110, f32[4,128,2048]{2,1,0:T(8,128)} %get-tuple-element.242, f32[4,128]{1,0:T(4,128)S(1)} %get-tuple-element.243), kind=kOutput, calls=%fused_computation.18.clone.1 | convolution fusion | flops 275843584 | bytes 10618880 | tf_op jit(solution)/shard_map/while/body/eval_jaxpr/htu,uhd->thd/dot_general | solution.py:81
  170.5 3.1 convolution_convert_fusion.2
  175.1 9.5 %fusion.114 = bf16[4,128,2048]{2,1,0:T(8,128)(2,1)} fusion(bf16[128,4,128]{0,2,1:T(8,128)(2,1)S(1)} %bitcast.144, f32[4,128,2048]{2,1,0:T(8,128)} %fusion.110, f32[4,128,2048]{2,1,0:T(8,128)} %get-tuple-element.242, f32[4,128]{1,0:T(4,128)S(1)} %get-tuple-element.243), kind=kOutput, calls=%fused_computation.10.clone.1 | convolution fusion | flops 275778048 | bytes 10618880 | tf_op jit(solution)/shard_map/while/body/eval_jaxpr/htu,thd->uhd/dot_general | solution.py:83
  184.6 4.0 constant_dynamic-update-slice_fusion.7
  189.8 3.2 constant_dynamic-slice_fusion.8
  199.7 6.5 %fusion.111 = (f32[4,128]{1,0:T(4,128)S(1)}, f32[4,128,2048]{2,1,0:T(8,128)}) fusion(pred[128,2048]{1,0:T(8,128)(4,1)S(1)} %iota_compare_fusion.2, bf16[128,4,128]{0,2,1:T(8,128)(2,1)S(1)} %bitcast.143, bf16[2048,4,128]{0,2,1:T(8,128)(2,1)} %bitcast.125), kind=kOutput, calls=%fused_computation.95.clone.1 | convolution fusion | flops 543164416 | bytes 6686720 | tf_op jit(solution)/shard_map/while/body/eval_jaxpr/sub | solution.py:70
  206.3 8.5 %fusion.112 = bf16[4,128,128]{2,1,0:T(8,128)(2,1)S(1)} fusion(bf16[2048,4,128]{0,2,1:T(8,128)(2,1)} %bitcast.126, f32[4,128,2048]{2,1,0:T(8,128)} %fusion.110, f32[4,128,2048]{2,1,0:T(8,128)} %get-tuple-element.242, f32[4,128]{1,0:T(4,128)S(1)} %get-tuple-element.243), kind=kOutput, calls=%fused_computation.18.clone.1 | convolution fusion | flops 275843584 | bytes 10618880 | tf_op jit(solution)/shard_map/while/body/eval_jaxpr/htu,uhd->thd/dot_general | solution.py:81
  219.4 9.5 %fusion.114 = bf16[4,128,2048]{2,1,0:T(8,128)(2,1)} fusion(bf16[128,4,128]{0,2,1:T(8,128)(2,1)S(1)} %bitcast.144, f32[4,128,2048]{2,1,0:T(8,128)} %fusion.110, f32[4,128,2048]{2,1,0:T(8,128)} %get-tuple-element.242, f32[4,128]{1,0:T(4,128)S(1)} %get-tuple-element.243), kind=kOutput, calls=%fused_computation.10.clone.1 | convolution fusion | flops 275778048 | bytes 10618880 | tf_op jit(solution)/shard_map/while/body/eval_jaxpr/htu,thd->uhd/dot_general | solution.py:83
  228.9 4.0 constant_dynamic-update-slice_fusion.7
  234.2 3.2 constant_dynamic-slice_fusion.8
  244.1 6.5 %fusion.111 = (f32[4,128]{1,0:T(4,128)S(1)}, f32[4,128,2048]{2,1,0:T(8,128)}) fusion(pred[128,2048]{1,0:T(8,128)(4,1)S(1)} %iota_compare_fusion.2, bf16[128,4,128]{0,2,1:T(8,128)(2,1)S(1)} %bitcast.143, bf16[2048,4,128]{0,2,1:T(8,128)(2,1)} %bitcast.125), kind=kOutput, calls=%fused_computation.95.clone.1 | convolution fusion | flops 543164416 | bytes 6686720 | tf_op jit(solution)/shard_map/while/body/eval_jaxpr/sub | solution.py:70
  250.6 8.5 %fusion.112 = bf16[4,128,128]{2,1,0:T(8,128)(2,1)S(1)} fusion(bf16[2048,4,128]{0,2,1:T(8,128)(2,1)} %bitcast.126, f32[4,128,2048]{2,1,0:T(8,128)} %fusion.110, f32[4,128,2048]{2,1,0:T(8,128)} %get-tuple-element.242, f32[4,128]{1,0:T(4,128)S(1)} %get-tuple-element.243), kind=kOutput, calls=%fused_computation.18.clone.1 | convolution fusion | flops 275843584 | bytes 10618880 | tf_op jit(solution)/shard_map/while/body/eval_jaxpr/htu,uhd->thd/dot_general | solution.py:81
  259.2 3.1 convolution_convert_fusion.2
  263.8 9.5 %fusion.114 = bf16[4,128,2048]{2,1,0:T(8,128)(2,1)} fusion(bf16[128,4,128]{0,2,1:T(8,128)(2,1)S(1)} %bitcast.144, f32[4,128,2048]{2,1,0:T(8,128)} %fusion.110, f32[4,128,2048]{2,1,0:T(8,128)} %get-tuple-element.242, f32[4,128]{1,0:T(4,128)S(1)} %get-tuple-element.243), kind=kOutput, calls=%fused_computation.10.clone.1 | convolution fusion | flops 275778048 | bytes 10618880 | tf_op jit(solution)/shard_map/while/body/eval_jaxpr/htu,thd->uhd/dot_general | solution.py:83
  273.3 4.0 constant_dynamic-update-slice_fusion.7
  278.5 3.2 constant_dynamic-slice_fusion.8
  288.4 6.5 %fusion.111 = (f32[4,128]{1,0:T(4,128)S(1)}, f32[4,128,2048]{2,1,0:T(8,128)}) fusion(pred[128,2048]{1,0:T(8,128)(4,1)S(1)} %iota_compare_fusion.2, bf16[128,4,128]{0,2,1:T(8,128)(2,1)S(1)} %bitcast.143, bf16[2048,4,128]{0,2,1:T(8,128)(2,1)} %bitcast.125), kind=kOutput, calls=%fused_computation.95.clone.1 | convolution fusion | flops 543164416 | bytes 6686720 | tf_op jit(solution)/shard_map/while/body/eval_jaxpr/sub | solution.py:70
  294.9 8.5 %fusion.112 = bf16[4,128,128]{2,1,0:T(8,128)(2,1)S(1)} fusion(bf16[2048,4,128]{0,2,1:T(8,128)(2,1)} %bitcast.126, f32[4,128,2048]{2,1,0:T(8,128)} %fusion.110, f32[4,128,2048]{2,1,0:T(8,128)} %get-tuple-element.242, f32[4,128]{1,0:T(4,128)S(1)} %get-tuple-element.243), kind=kOutput, calls=%fused_computation.18.clone.1 | convolution fusion | flops 275843584 | bytes 10618880 | tf_op jit(solution)/shard_map/while/body/eval_jaxpr/htu,uhd->thd/dot_general | solution.py:81
  303.5 3.1 convolution_convert_fusion.2
  308.1 9.5 %fusion.114 = bf16[4,128,2048]{2,1,0:T(8,128)(2,1)} fusion(bf16[128,4,128]{0,2,1:T(8,128)(2,1)S(1)} %bitcast.144, f32[4,128,2048]{2,1,0:T(8,128)} %fusion.110, f32[4,128,2048]{2,1,0:T(8,128)} %get-tuple-element.242, f32[4,128]{1,0:T(4,128)S(1)} %get-tuple-element.243), kind=kOutput, calls=%fused_computation.10.clone.1 | convolution fusion | flops 275778048 | bytes 10618880 | tf_op jit(solution)/shard_map/while/body/eval_jaxpr/htu,thd->uhd/dot_general | solution.py:83
  317.6 4.0 constant_dynamic-update-slice_fusion.7
  321.6 14.6 %copy.60 = bf16[4,2048,512]{2,0,1:T(4,128)(2,1)} copy(bf16[4,2048,512]{1,2,0:T(8,128)(2,1)} %get-tuple-element.67) | data formatting | bytes 16777216
  336.2 10.2 %copy.65 = bf16[256,8,4,512]{3,1,2,0:T(8,128)(2,1)} copy(bf16[256,8,4,512]{3,2,1,0:T(4,128)(2,1)} %bitcast.131) | data formatting | bytes 16777216
  346.5 14.6 %copy.62 = bf16[4,2048,512]{2,0,1:T(4,128)(2,1)} copy(bf16[4,2048,512]{1,2,0:T(8,128)(2,1)} %get-tuple-element.68) | data formatting | bytes 16777216
  361.0 10.2 %copy.66 = bf16[256,8,4,512]{3,1,2,0:T(8,128)(2,1)} copy(bf16[256,8,4,512]{3,2,1,0:T(4,128)(2,1)} %bitcast.132) | data formatting | bytes 16777216
  379.1 78.2 %psum.7 = f32[7,2048]{1,0:T(8,128)} all-reduce(f32[7,2048]{1,0:T(8,128)S(1)} %stack.31), channel_id=1, replica_groups=mesh['dp'=16,'seq'=16] {'dp','seq'}, use_global_device_ids=true, to_apply=%region_14.15 | all-reduce | flops 14336 | bytes 114688 | tf_op jit(solution)/shard_map/psum | solution.py:116
  462.0 86.5 %reduce-scatter.9.cloned.1.call-done = bf16[128,2048]{1,0:T(8,128)(2,1)} async-done(((bf16[2048,2048]{1,0:T(8,128)(2,1)}), bf16[128,2048]{1,0:T(8,128)(2,1)}) %reduce-scatter.9.cloned.1.call-update) | async-done | bytes 524304
  (123 shorter events, 66.9 us)
Async XLA Ops:
  7.2 11.9 %copy-start = (bf16[1,128,2048]{2,1,0:T(8,128)(2,1)S(1)}, bf16[1,128,2048]{2,1,0:T(8,128)(2,1)}, u32[]{:S(2)}) copy-start(bf16[1,128,2048]{2,1,0:T(8,128)(2,1)} %param.10) | copy-start | bytes 1572868
  7.2 71.6 %all-gather.5.cloned.1.call-start = ((), (), s32[]{:S(2)}) async-start(), calls=%async_computation.2 | async-start | bytes 8912896 | tf_op jit(solution)/shard_map/all_gather | solution.py:49
  9.3 134.8 %all-gather.7.cloned.1.call-start = ((), (), s32[]{:S(2)}) async-start(), calls=%async_computation.3 | async-start | bytes 8912896 | tf_op jit(solution)/shard_map/all_gather | solution.py:48
  11.5 447.6 %reduce-scatter.7.cloned.1.call-start = ((), (), s32[]{:S(2)}) async-start(), calls=%async_computation.4 | async-start | bytes 8912896
  12.3 6.8 %collective-permute-start.1 = (bf16[3,2048]{1,0:T(4,128)(2,1)S(1)}, bf16[3,2048]{1,0:T(4,128)(2,1)S(1)}, u32[]{:S(2)}, u32[]{:S(2)}) collective-permute-start(bf16[3,2048]{1,0:T(4,128)(2,1)S(1)} %get-tuple-element.161), channel_id=1, source_target_pairs={{0,1},{1,2},{2,3},{3,4},{4,5},{5,6},{6,7},{7,8},{8,9},{9,10},{10,1... | collective-permute-start | bytes 36872 | tf_op jit(solution)/shard_map/ppermute | solution.py:18
  15.1 4.0 collective-permute-start
  16.9 127.2 %copy-start.2 = (f32[1,2048]{1,0:T(1,128)}, f32[1,2048]{1,0:T(1,128)S(1)}, u32[]{:S(2)}) copy-start(f32[1,2048]{1,0:T(1,128)S(1)} %get-tuple-element.162) | copy-start | bytes 24580
  16.9 127.2 %copy-start.4 = (f32[1,2048]{1,0:T(1,128)}, f32[1,2048]{1,0:T(1,128)S(1)}, u32[]{:S(2)}) copy-start(f32[1,2048]{1,0:T(1,128)S(1)} %get-tuple-element.163) | copy-start | bytes 24580
  16.9 127.2 %copy-start.6 = (f32[1,2048]{1,0:T(1,128)}, f32[1,2048]{1,0:T(1,128)S(1)}, u32[]{:S(2)}) copy-start(f32[1,2048]{1,0:T(1,128)S(1)} %get-tuple-element.164) | copy-start | bytes 24580
  17.0 127.2 %copy-start.8 = (f32[1,2048]{1,0:T(1,128)}, f32[1,2048]{1,0:T(1,128)S(1)}, u32[]{:S(2)}) copy-start(f32[1,2048]{1,0:T(1,128)S(1)} %get-tuple-element.165) | copy-start | bytes 24580
  17.0 127.2 %copy-start.10 = (f32[1,2048]{1,0:T(1,128)}, f32[1,2048]{1,0:T(1,128)S(1)}, u32[]{:S(2)}) copy-start(f32[1,2048]{1,0:T(1,128)S(1)} %get-tuple-element.166) | copy-start | bytes 24580
  17.0 127.2 %copy-start.12 = (f32[1,2048]{1,0:T(1,128)}, f32[1,2048]{1,0:T(1,128)S(1)}, u32[]{:S(2)}) copy-start(f32[1,2048]{1,0:T(1,128)S(1)} %get-tuple-element.167) | copy-start | bytes 24580
  17.0 127.2 %copy-start.14 = (f32[1,2048]{1,0:T(1,128)}, f32[1,2048]{1,0:T(1,128)S(1)}, u32[]{:S(2)}) copy-start(f32[1,2048]{1,0:T(1,128)S(1)} %get-tuple-element.168) | copy-start | bytes 24580
  170.5 3.8 copy-start.16
  214.8 3.8 copy-start.16
  259.1 3.8 copy-start.16
  303.5 3.8 copy-start.16
  346.4 202.0 %reduce-scatter.9.cloned.1.call-start = ((), (), s32[]{:S(2)}) async-start(), calls=%async_computation.5 | async-start | bytes 8912896
  371.3 1.0 copy-start.1
  372.5 84.8 %copy-start.3 = (f32[1,2048]{1,0:T(1,128)S(1)}, f32[1,2048]{1,0:T(1,128)}, u32[]{:S(2)}) copy-start(f32[1,2048]{1,0:T(1,128)} %copy-done.2) | copy-start | bytes 24580
  372.5 84.8 %copy-start.5 = (f32[1,2048]{1,0:T(1,128)S(1)}, f32[1,2048]{1,0:T(1,128)}, u32[]{:S(2)}) copy-start(f32[1,2048]{1,0:T(1,128)} %copy-done.4) | copy-start | bytes 24580
  372.6 84.8 %copy-start.7 = (f32[1,2048]{1,0:T(1,128)S(1)}, f32[1,2048]{1,0:T(1,128)}, u32[]{:S(2)}) copy-start(f32[1,2048]{1,0:T(1,128)} %copy-done.6) | copy-start | bytes 24580
  372.6 84.7 %copy-start.9 = (f32[1,2048]{1,0:T(1,128)S(1)}, f32[1,2048]{1,0:T(1,128)}, u32[]{:S(2)}) copy-start(f32[1,2048]{1,0:T(1,128)} %copy-done.8) | copy-start | bytes 24580
  372.6 84.7 %copy-start.11 = (f32[1,2048]{1,0:T(1,128)S(1)}, f32[1,2048]{1,0:T(1,128)}, u32[]{:S(2)}) copy-start(f32[1,2048]{1,0:T(1,128)} %copy-done.10) | copy-start | bytes 24580
  372.6 84.7 %copy-start.13 = (f32[1,2048]{1,0:T(1,128)S(1)}, f32[1,2048]{1,0:T(1,128)}, u32[]{:S(2)}) copy-start(f32[1,2048]{1,0:T(1,128)} %copy-done.12) | copy-start | bytes 24580
  372.6 84.7 %copy-start.15 = (f32[1,2048]{1,0:T(1,128)S(1)}, f32[1,2048]{1,0:T(1,128)}, u32[]{:S(2)}) copy-start(f32[1,2048]{1,0:T(1,128)} %copy-done.14) | copy-start | bytes 24580
  373.0 4.9 collective-permute-start.3
  373.7 4.3 collective-permute-start.2
Sparse Core Ops, SparseCore 0:
  10.4 68.3 all-gather.4
  81.1 63.0 all-gather.6
  346.6 99.6 reduce-scatter.6
  448.7 99.6 reduce-scatter.8
where the time goes:
time: 560 us; the launch traced here: 558 us
  waiting for transfers between devices  210 us (38%)
  matrix products  125 us (22%)
  local copies, waits for them, and re-layouts  116 us (21%)
  blocking collectives  78.2 us (14%)
  between operations  14.1 us (3%)
  other arithmetic  5.7 us (1%)
  starting transfers between devices  5.66 us (1%)
    unnamed x6, waiting for transfers between devices  86.6 us
    psum x1, blocking collectives, on_device(): filter_gradient = lax.psum(jnp.stack(filter_rows, 0), ('dp', 'seq'))  78.2 us
    all_gather x1, waiting for transfers between devices, on_device(): lax.all_gather(local_k, 'seq', axis=0, tiled=True)  65.4 us
    unnamed x46, local copies, waits for them, and re-layouts  62.6 us
    all_gather x1, waiting for transfers between devices, on_device(): lax.all_gather(local_v, 'seq', axis=0, tiled=True)  57.9 us
    dot_general x4, matrix products, forward_group(): jnp.einsum('htu,thd->uhd', dscore, q_part, preferred_element_type=jnp.flo...  38 us
    dot_general x4, matrix products, forward_group(): jnp.einsum('htu,uhd->thd', dscore, k_part, preferred_element_type=jnp.flo...  34.2 us
    dynamic_slice x20, local copies, waits for them, and re-layouts, columns(): lax.dynamic_slice_in_dim(matrix, group_index * group_width, group_width, 1)  27.5 us
  transfers between devices with their start and end apart: 8, of which 3 were waited for; matrix products, arithmetic and copies ran while one was open for 7% of the time, Pallas kernels for 0%

commit v1 on v0

--- a/solution.py
+++ b/solution.py
@@ -1,3 +1,4 @@
+import functools
 import math
 import jax
 import jax.numpy as jnp
@@ -6,6 +7,14 @@
 
 HD = 128
 TAPS = 7
+
+
+def make_run(page, chip_axis):
+    all_rows = jnp.sum(lax.all_gather(page, axis_name=chip_axis), axis=0)
+    return all_rows
+
+
+push_ladders_in = functools.partial(make_run, chip_axis=("dp", "seq"))
 
 
 def padded(value, sides, width):
@@ -113,7 +122,7 @@
         moved = out_pad[tap_index : tap_index + tok_rows].astype(jnp.float32)
         conv_sum = conv_sum + filter_taps[tap_index] * moved
         filter_rows.append(jnp.sum(moved * local_gf, 0))
-    filter_gradient = lax.psum(jnp.stack(filter_rows, 0), ("dp", "seq"))
+    filter_gradient = push_ladders_in(jnp.stack(filter_rows, 0))
     conv_output = conv_sum.astype(jnp.bfloat16)
     return (
         conv_output[None],

time: 560 us -> 995 us (1.78)
  waiting for transfers between devices: 210 us -> 716 us
  blocking collectives: 78.2 us -> 0 us
    all_gather x0 -> x1, waiting for transfers between devices: none -> 430 us  [make_run(): all_rows = jnp.sum(lax.all_gather(page, axis_name=chip_axis), axis=0)]
    psum x1 -> x0, blocking collectives: 78.2 us -> none  [on_device(): filter_gradient = lax.psum(jnp.stack(filter_rows, 0), ('dp', 'seq'))]
    unnamed x6 -> x7, waiting for transfers between devices: 86.6 us -> 163 us
    unnamed x46 -> x48, local copies, waits for them, and re-layouts: 62.6 us -> 62.5 us
  transfers between devices with their start and end apart: 8 -> 9, of which waited for: 3 -> 6; matrix products, arithmetic and copies ran while one was open for 7% -> 4% of each run, Pallas kernels for 0% -> 0%
where the time goes in v1:
time: 995 us; the launch traced here: 993 us
  waiting for transfers between devices  716 us (72%)
  matrix products  125 us (13%)
  local copies, waits for them, and re-layouts  116 us (12%)
  between operations  14.1 us (1%)
  other arithmetic  13.3 us (1%)
    all_gather x1, waiting for transfers between devices, make_run(): all_rows = jnp.sum(lax.all_gather(page, axis_name=chip_axis), axis=0)  430 us
    unnamed x7, waiting for transfers between devices  163 us
    all_gather x1, waiting for transfers between devices, on_device(): lax.all_gather(local_k, 'seq', axis=0, tiled=True)  65.4 us
    unnamed x48, local copies, waits for them, and re-layouts  62.5 us
    all_gather x1, waiting for transfers between devices, on_device(): lax.all_gather(local_v, 'seq', axis=0, tiled=True)  57.9 us
    dot_general x4, matrix products, forward_group(): jnp.einsum('htu,thd->uhd', dscore, q_part, preferred_element_type=jnp.flo...  38 us
    dot_general x4, matrix products, forward_group(): jnp.einsum('htu,uhd->thd', dscore, k_part, preferred_element_type=jnp.flo...  34.2 us
    dynamic_slice x20, local copies, waits for them, and re-layouts, columns(): lax.dynamic_slice_in_dim(matrix, group_index * group_width, group_width, 1)  27.5 us
  transfers between devices with their start and end apart: 9, of which 6 were waited for; matrix products, arithmetic and copies ran while one was open for 4% of the time, Pallas kernels for 0%

profile of v1, /device:TPU:1, one launch (start us, length us, event | category | flops | bytes accessed | tf_op | source)
XLA Modules:
  0.0 993.2 jit_solution(4219799679103300817)
XLA Ops:
  20.9 57.9 %all-gather.8.cloned.1.call-done = bf16[1,2048,2048]{1,2,0:T(8,128)(2,1)} async-done(((bf16[1,128,2048]{1,2,0:T(8,128)(2,1)}), bf16[1,2048,2048]{1,2,0:T(8,128)(2,1)}) %all-gather.8.cloned.1.call-update) | async-done | bytes 8388624 | tf_op jit(solution)/shard_map/all_gather | solution.py:58
  78.7 65.4 %all-gather.10.cloned.1.call-done = bf16[1,2048,2048]{1,2,0:T(8,128)(2,1)} async-done(((bf16[1,128,2048]{1,2,0:T(8,128)(2,1)}), bf16[1,2048,2048]{1,2,0:T(8,128)(2,1)}) %all-gather.10.cloned.1.call-update) | async-done | bytes 8388624 | tf_op jit(solution)/shard_map/all_gather | solution.py:57
  144.2 177.3 %while.17 = (s32[]{:T(128)}, bf16[4,128,512]{1,2,0:T(8,128)(2,1)S(1)}, bf16[4,128,512]{1,2,0:T(8,128)(2,1)}, bf16[4,2048,512]{1,2,0:T(8,128)(2,1)}, bf16[4,2048,...) while((s32[]{:T(128)}, ...), condition=%wide.region_4.5_spmd.clone, body=%wide.region_0.4_spmd.clone.sunk | while | flops 1904614400 | bytes 82324224 | solution.py:104
  145.5 3.2 constant_dynamic-slice_fusion.8
  155.4 6.5 fusion.111
  161.9 8.5 fusion.112
  175.1 9.5 fusion.114
  184.6 4.0 constant_dynamic-update-slice_fusion.7
  189.8 3.2 constant_dynamic-slice_fusion.8
  199.7 6.5 fusion.111
  206.2 8.5 fusion.112
  219.4 9.5 fusion.114
  228.9 4.0 constant_dynamic-update-slice_fusion.7
  234.1 3.2 constant_dynamic-slice_fusion.8
  244.1 6.5 fusion.111
  250.6 8.5 fusion.112
  263.7 9.5 fusion.114
  273.2 4.0 constant_dynamic-update-slice_fusion.7
  278.4 3.2 constant_dynamic-slice_fusion.8
  288.3 6.5 fusion.111
  294.8 8.5 fusion.112
  303.4 3.1 convolution_convert_fusion.2
  308.0 9.5 fusion.114
  317.5 4.0 constant_dynamic-update-slice_fusion.7
  321.5 14.5 %copy.60 = bf16[4,2048,512]{2,0,1:T(4,128)(2,1)} copy(bf16[4,2048,512]{1,2,0:T(8,128)(2,1)} %get-tuple-element.67) | data formatting | bytes 16777216
  336.0 10.2 %copy.65 = bf16[256,8,4,512]{3,1,2,0:T(8,128)(2,1)} copy(bf16[256,8,4,512]{3,2,1,0:T(4,128)(2,1)} %bitcast.132) | data formatting | bytes 16777216
  346.3 14.6 %copy.62 = bf16[4,2048,512]{2,0,1:T(4,128)(2,1)} copy(bf16[4,2048,512]{1,2,0:T(8,128)(2,1)} %get-tuple-element.68) | data formatting | bytes 16777216
  360.9 10.2 %copy.66 = bf16[256,8,4,512]{3,1,2,0:T(8,128)(2,1)} copy(bf16[256,8,4,512]{3,2,1,0:T(4,128)(2,1)} %bitcast.133) | data formatting | bytes 16777216
  381.0 64.5 %reduce-scatter.7.cloned.1.call-done = bf16[128,2048]{1,0:T(8,128)(2,1)} async-done(((bf16[2048,2048]{1,0:T(8,128)(2,1)}), bf16[128,2048]{1,0:T(8,128)(2,1)}) %reduce-scatter.7.cloned.1.call-update) | async-done | bytes 524304
  448.3 98.4 %reduce-scatter.9.cloned.1.call-done = bf16[128,2048]{1,0:T(8,128)(2,1)} async-done(((bf16[2048,2048]{1,0:T(8,128)(2,1)}), bf16[128,2048]{1,0:T(8,128)(2,1)}) %reduce-scatter.9.cloned.1.call-update) | async-done | bytes 524304
  549.5 429.5 %all-gather.12.cloned.1.call-done = f32[256,7,2048]{2,1,0:T(8,128)} async-done(((f32[1,7,2048]{2,1,0:T(8,128)}), f32[256,7,2048]{2,1,0:T(8,128)}) %all-gather.12.cloned.1.call-update) | async-done | bytes 14680080 | tf_op jit(solution)/shard_map/all_gather | solution.py:13
  979.1 7.6 reduce_sum.97
  (128 shorter events, 73.3 us)
Async XLA Ops:
  7.2 11.9 %copy-start = (bf16[1,128,2048]{2,1,0:T(8,128)(2,1)S(1)}, bf16[1,128,2048]{2,1,0:T(8,128)(2,1)}, u32[]{:S(2)}) copy-start(bf16[1,128,2048]{2,1,0:T(8,128)(2,1)} %param.10) | copy-start | bytes 1572868
  7.2 71.6 %all-gather.8.cloned.1.call-start = ((), (), s32[]{:S(2)}) async-start(), calls=%async_computation.2 | async-start | bytes 8912896 | tf_op jit(solution)/shard_map/all_gather | solution.py:58
  9.3 134.8 %all-gather.10.cloned.1.call-start = ((), (), s32[]{:S(2)}) async-start(), calls=%async_computation.3 | async-start | bytes 8912896 | tf_op jit(solution)/shard_map/all_gather | solution.py:57
  11.5 434.0 %reduce-scatter.7.cloned.1.call-start = ((), (), s32[]{:S(2)}) async-start(), calls=%async_computation.5 | async-start | bytes 8912896
  12.3 6.8 collective-permute-start.1
  15.1 4.0 collective-permute-start
  16.9 127.2 %copy-start.3 = (f32[1,2048]{1,0:T(1,128)}, f32[1,2048]{1,0:T(1,128)S(1)}, u32[]{:S(2)}) copy-start(f32[1,2048]{1,0:T(1,128)S(1)} %get-tuple-element.162) | copy-start | bytes 24580
  16.9 127.2 %copy-start.5 = (f32[1,2048]{1,0:T(1,128)}, f32[1,2048]{1,0:T(1,128)S(1)}, u32[]{:S(2)}) copy-start(f32[1,2048]{1,0:T(1,128)S(1)} %get-tuple-element.163) | copy-start | bytes 24580
  16.9 127.2 %copy-start.7 = (f32[1,2048]{1,0:T(1,128)}, f32[1,2048]{1,0:T(1,128)S(1)}, u32[]{:S(2)}) copy-start(f32[1,2048]{1,0:T(1,128)S(1)} %get-tuple-element.164) | copy-start | bytes 24580
  17.0 127.2 %copy-start.9 = (f32[1,2048]{1,0:T(1,128)}, f32[1,2048]{1,0:T(1,128)S(1)}, u32[]{:S(2)}) copy-start(f32[1,2048]{1,0:T(1,128)S(1)} %get-tuple-element.165) | copy-start | bytes 24580
  17.0 127.2 %copy-start.11 = (f32[1,2048]{1,0:T(1,128)}, f32[1,2048]{1,0:T(1,128)S(1)}, u32[]{:S(2)}) copy-start(f32[1,2048]{1,0:T(1,128)S(1)} %get-tuple-element.166) | copy-start | bytes 24580
  17.0 127.2 %copy-start.13 = (f32[1,2048]{1,0:T(1,128)}, f32[1,2048]{1,0:T(1,128)S(1)}, u32[]{:S(2)}) copy-start(f32[1,2048]{1,0:T(1,128)S(1)} %get-tuple-element.167) | copy-start | bytes 24580
  17.0 127.2 %copy-start.15 = (f32[1,2048]{1,0:T(1,128)}, f32[1,2048]{1,0:T(1,128)S(1)}, u32[]{:S(2)}) copy-start(f32[1,2048]{1,0:T(1,128)S(1)} %get-tuple-element.168) | copy-start | bytes 24580
  170.4 3.8 copy-start.17
  214.8 3.8 copy-start.17
  259.1 3.8 copy-start.17
  303.4 3.8 copy-start.17
  346.3 200.4 %reduce-scatter.9.cloned.1.call-start = ((), (), s32[]{:S(2)}) async-start(), calls=%async_computation.6 | async-start | bytes 8912896
  371.2 1.0 copy-start.1
  371.2 607.9 %all-gather.12.cloned.1.call-start = ((), (), s32[]{:S(2)}) async-start(), calls=%async_computation.4 | async-start | bytes 16842752 | tf_op jit(solution)/shard_map/all_gather | solution.py:13
  372.4 6.8 copy-start.4
  372.4 6.8 copy-start.6
  372.4 6.8 copy-start.8
  372.4 6.8 copy-start.10
  372.5 6.7 copy-start.12
  372.5 6.7 copy-start.14
  372.5 6.7 copy-start.16
  372.9 5.2 copy-start.2
  372.9 3.5 collective-permute-start.3
  373.6 2.8 collective-permute-start.2
Sparse Core Ops, SparseCore 0:
  10.4 68.3 all-gather.7
  81.1 63.0 all-gather.9
  346.4 98.9 reduce-scatter.6
  447.8 98.8 reduce-scatter.8
  549.0 430.0 all-gather.11
